TPU v7x, 128 devices: a whole 4x4x4 slice. The times are simulated.
128 devices in a mesh: seq: 32 (over x, z, core), mp: 4 (over y).
Axes of the slice: x: 4, y: 4, z: 4, core: 2. Of those that a mesh axis runs over, the one named last changes fastest.
Arguments:
- hidden: bfloat16 [16384, 4096], P('seq', 'mp'), may hold values from -6 to 6
- w_zx: bfloat16 [4096, 2, 4096], P(None, None, 'mp'), may hold values from -0.09375 to 0.09375
- w_bc: bfloat16 [4096, 2, 512], P(None, None, 'mp'), may hold values from -0.09375 to 0.09375
- w_dt: bfloat16 [4096, 64], P(None, 'mp'), may hold values from -0.09375 to 0.09375
- conv_x: float32 [4, 4096], P(None, 'mp'), may hold values from -3 to 3
- conv_x_bias: float32 [4096], P('mp'), may hold values from -3 to 3
- conv_bc: float32 [4, 2, 512], P(None, None, 'mp'), may hold values from -3 to 3
- conv_bc_bias: float32 [2, 512], P(None, 'mp'), may hold values from -3 to 3
- a_log: float32 [64], P('mp'), may hold values from -9.5 to -0.5
- dt_bias: float32 [64], P('mp'), may hold values from -4 to -1
- d_skip: float32 [64], P('mp'), may hold values from 0.5 to 4
- norm_gain: float32 [4096], P('mp'), may hold values from 0.4 to 1.6
- state_bank: float32 [2, 64, 64, 128], P(None, 'mp'), may hold values from -2 to 2
- conv_bank_x: bfloat16 [2, 3, 4096], P(None, None, 'mp'), may hold values from -5 to 5
- conv_bank_bc: bfloat16 [2, 3, 2, 512], P(None, None, None, 'mp'), may hold values from -5 to 5
- prompt_blocks: int32 [9], replicated, may hold values from 1 to 48, 64 in all
- prompt_order: int32 [9], replicated, may hold values from 0 to 8, each once
- resume_slot: int32 [9], replicated, may hold values from 0 to 2
Outputs:
- mixed: bfloat16 [16384, 4096], P('seq', 'mp')
Inputs may be any that keep to these rules, and one draw needn't show every extreme that they name: `prompt_blocks`: blocks of each prompt; they sum to 64 and the longest is exactly 48. `prompt_order`: A permutation of the prompts. `resume_slot`: 2 means a fresh start from zero state and zero convolution rows.
All inputs are finite; a program needn't handle non-finite values.
Results may differ from a plain program's by a relative error of at most 0.0068.
Values may be sent and summed in bfloat16 or wider, within the bound.
No kernel may reach another device: no remote copies, remote signals or barrier semaphores. Data moves between devices by JAX's collectives and lax.ppermute only.
A program may use at most 192 MiB of HBM per device.

v0:
```python
import jax
import jax.numpy as jnp
from jax import lax
from jax.sharding import PartitionSpec as P

WIDTH = 4096
HEAD_DIM = 64
STATE = 128
BLOCK = 256
KERNEL = 4
BANK = 2


def from_behind(value, axis, steps):
    count = lax.axis_size(axis)
    pairs = [(source, (source + steps) % count) for source in range(count)]
    return lax.ppermute(value, axis, pairs)


def combine(earlier, later):
    return (earlier[0] * later[0], later[0][:, None, None] * earlier[1] + later[1])


def per_device(
    hidden,
    w_zx,
    w_bc,
    w_dt,
    conv_x,
    conv_x_bias,
    conv_bc,
    conv_bc_bias,
    a_log,
    dt_bias,
    d_skip,
    norm_gain,
    state_bank,
    conv_bank_x,
    conv_bank_bc,
    prompt_blocks,
    prompt_order,
    resume_slot,
):
    devices = lax.axis_size("seq")
    place = lax.axis_index("seq")
    rows_dev = hidden.shape[0]
    blocks = rows_dev // BLOCK
    inner_dev = w_zx.shape[2]
    gstate_dev = w_bc.shape[2]
    heads_dev = w_dt.shape[1]
    groups_dev = gstate_dev // STATE
    per_group = heads_dev // groups_dev
    channels = inner_dev + 2 * gstate_dev
    prompts = prompt_blocks.shape[0]
    flat_zx = w_zx.reshape(WIDTH, 2 * inner_dev)
    flat_bc = w_bc.reshape(WIDTH, 2 * gstate_dev)
    piece = lax.all_gather(hidden, "mp", axis=1, tiled=True)
    zx_sum = jnp.dot(piece, flat_zx, preferred_element_type=jnp.float32)
    bc_sum = jnp.dot(piece, flat_bc, preferred_element_type=jnp.float32)
    dt_raw = jnp.dot(piece, w_dt, preferred_element_type=jnp.float32)
    zx = zx_sum.astype(jnp.bfloat16)
    bc = bc_sum.astype(jnp.bfloat16)
    gate = zx[:, :inner_dev]
    mixin = jnp.concatenate([zx[:, inner_dev:], bc], axis=1).reshape(blocks, BLOCK, channels)
    own_tails = mixin[:, BLOCK - (KERNEL - 1) :, :]
    arrived = from_behind(own_tails, "seq", 1)
    wrapped = jnp.concatenate([jnp.zeros_like(arrived[:1]), arrived[:-1]], axis=0)
    before = jnp.where(place > 0, arrived, wrapped)
    prompt_ids = jnp.arange(prompts, dtype=jnp.int32)
    order_hot = (prompt_order[:, None] == prompt_ids[None, :]).astype(jnp.int32)
    lengths = jnp.sum(order_hot * prompt_blocks[None, :], axis=1)
    slots = jnp.sum(order_hot * resume_slot[None, :], axis=1)
    ends = jnp.cumsum(lengths)
    starts = ends - lengths
    stream_ids = jnp.arange(blocks, dtype=jnp.int32) * devices + place
    inside = (
        (stream_ids[:, None] >= starts[None, :]) & (stream_ids[:, None] < ends[None, :])
    ).astype(jnp.int32)
    block_slot = jnp.sum(inside * slots[None, :], axis=1)
    first = jnp.any(stream_ids[:, None] == starts[None, :], axis=1)
    pick = (block_slot[:, None] == jnp.arange(BANK, dtype=jnp.int32)[None, :]).astype(jnp.float32)
    bank_state = jnp.einsum("cr,rhpn->chpn", pick, state_bank, precision=lax.Precision.HIGHEST)
    bank_rows = jnp.concatenate(
        [conv_bank_x, conv_bank_bc.reshape(BANK, KERNEL - 1, 2 * gstate_dev)], axis=2
    )
    bank_tail = jnp.einsum("cr,rkz->ckz", pick, bank_rows.astype(jnp.float32)).astype(jnp.bfloat16)
    tail = jnp.where(first[:, None, None], bank_tail, before)
    kernel = jnp.concatenate([conv_x, conv_bc.reshape(KERNEL, 2 * gstate_dev)], axis=1)
    bias = jnp.concatenate([conv_x_bias, conv_bc_bias.reshape(2 * gstate_dev)], axis=0)
    padded = jnp.concatenate([tail, mixin], axis=1).astype(jnp.float32)
    acc = bias[None, None, :] + padded[:, 0:BLOCK] * kernel[0]
    for k in range(1, KERNEL):
        acc = acc + padded[:, k : k + BLOCK] * kernel[k]
    conv = jax.nn.silu(acc).astype(jnp.bfloat16)
    xs = conv[..., :inner_dev].reshape(blocks, BLOCK, groups_dev, per_group, HEAD_DIM)
    bs = conv[..., inner_dev : inner_dev + gstate_dev].reshape(blocks, BLOCK, groups_dev, STATE)
    cq = conv[..., inner_dev + gstate_dev :].reshape(blocks, BLOCK, groups_dev, STATE)
    dt = jax.nn.softplus(dt_raw.reshape(blocks, BLOCK, heads_dev) + dt_bias[None, None, :])
    cum = jnp.cumsum(dt * (-jnp.exp(a_log))[None, None, :], axis=1)
    scores = jnp.einsum("cqgn,ckgn->cgqk", cq, bs, preferred_element_type=jnp.float32)
    cum_h = cum.transpose(0, 2, 1)
    lower = jnp.arange(BLOCK)[:, None] >= jnp.arange(BLOCK)[None, :]
    damp = jnp.exp(
        jnp.where(lower[None, None], cum_h[:, :, :, None] - cum_h[:, :, None, :], -jnp.inf)
    )
    damp = damp.reshape(blocks, groups_dev, per_group, BLOCK, BLOCK)
    dt_h = dt.transpose(0, 2, 1).reshape(blocks, groups_dev, per_group, 1, BLOCK)
    mix = (scores[:, :, None] * damp * dt_h).astype(jnp.bfloat16)
    y_intra = jnp.einsum("cgjqk,ckgjp->cqgjp", mix, xs, preferred_element_type=jnp.float32)
    last = cum[:, -1, :]
    grow = jnp.exp(last)
    factor = (dt * jnp.exp(last[:, None, :] - cum)).reshape(blocks, BLOCK, groups_dev, per_group, 1)
    weighted = (xs.astype(jnp.float32) * factor).astype(jnp.bfloat16)
    local_state = jnp.einsum(
        "cqgjp,cqgn->cgjpn", weighted, bs, preferred_element_type=jnp.float32
    ).reshape(blocks, heads_dev, HEAD_DIM, STATE)
    step_a = jnp.where(first[:, None], 0.0, grow)
    step_b = local_state + jnp.where(
        first[:, None, None, None], grow[:, :, None, None] * bank_state, 0.0
    )
    core = place % 2
    chip = place // 2
    chips = devices // 2
    half = heads_dev // 2
    rows = blocks * half

    def keep(part, at):
        piece = lax.dynamic_slice_in_dim(part, at * half, half, axis=1)
        return piece.reshape((rows,) + part.shape[2:])

    pair = [(source, source ^ 1) for source in range(devices)]
    mine = (keep(step_a, core), keep(step_b, core))
    got = lax.ppermute((keep(step_a, 1 - core), keep(step_b, 1 - core)), "seq", pair)
    early = jax.tree.map(lambda own, other: jnp.where(core == 0, own, other), mine, got)
    later = jax.tree.map(lambda own, other: jnp.where(core == 0, other, own), mine, got)
    quarter = half // 2
    split_heads = lambda part: [
        part.reshape((blocks, 2, quarter) + part.shape[1:])[:, g].reshape(
            (blocks * quarter,) + part.shape[1:]
        )
        for g in range(2)
    ]
    chip_a, chip_b = combine(early, later)
    lanes = [list(pair) for pair in zip(split_heads(chip_a), split_heads(chip_b))]
    priors = [[jnp.ones_like(lane[0]), jnp.zeros_like(lane[1])] for lane in lanes]

    def wrap(part, neutral, late):
        moved = jnp.concatenate(
            [jnp.full_like(part[:quarter], neutral), part[: part.shape[0] - quarter]], axis=0
        )
        return jnp.where(late, part, moved)

    span = 1
    while span < chips:
        late = chip >= span
        for g in range(2):
            got_a, got_b = from_behind(tuple(lanes[g]), "seq", 2 * span)
            lead = (wrap(got_a, 1.0, late), wrap(got_b, 0.0, late))
            lanes[g] = list(combine(lead, tuple(lanes[g])))
            priors[g] = list(combine(lead, tuple(priors[g])))
        span *= 2
    joined = []
    for g in range(2):
        run_a, run_b = lanes[g]
        prior_a, prior_b = priors[g]
        lift = combine((run_a[:quarter], run_b[:quarter]), (prior_a[quarter:], prior_b[quarter:]))[
            1
        ]
        joined.append(jnp.concatenate([prior_b[:quarter], lift], axis=0))
    before_chip = jnp.concatenate(
        [part.reshape((blocks, quarter) + part.shape[1:]) for part in joined], axis=1
    ).reshape(chip_b.shape)
    after_early = early[0][:, None, None] * before_chip + early[1]
    own_part = jnp.where(core == 0, before_chip, after_early)
    other_part = lax.ppermute(jnp.where(core == 0, after_early, before_chip), "seq", pair)
    split_rows = lambda part: part.reshape((blocks, half) + part.shape[1:])
    own_part, other_part = (split_rows(own_part), split_rows(other_part))
    previous = jnp.where(
        core == 0,
        jnp.concatenate([own_part, other_part], axis=1),
        jnp.concatenate([other_part, own_part], axis=1),
    )
    state_in = jnp.where(first[:, None, None, None], bank_state, previous)
    read = jnp.einsum(
        "cqgn,cgjpn->cqgjp",
        cq.astype(jnp.float32),
        state_in.reshape(blocks, groups_dev, per_group, HEAD_DIM, STATE),
        precision=lax.Precision.HIGHEST,
    )
    growth = jnp.exp(cum).reshape(blocks, BLOCK, groups_dev, per_group, 1)
    skip = d_skip.reshape(1, 1, groups_dev, per_group, 1)
    y_total = y_intra + growth * read + skip * xs.astype(jnp.float32)
    gated = y_total.reshape(rows_dev, inner_dev) * jax.nn.silu(gate.astype(jnp.float32))
    grouped = gated.reshape(rows_dev, groups_dev, inner_dev // groups_dev)
    scale = lax.rsqrt(jnp.mean(grouped * grouped, axis=2, keepdims=True) + 1e-05)
    result = (grouped * scale).reshape(rows_dev, inner_dev) * norm_gain[None, :]
    return result.astype(jnp.bfloat16)


def solution(mesh):
    placed = (
        P("seq", "mp"),
        P(None, None, "mp"),
        P(None, None, "mp"),
        P(None, "mp"),
        P(None, "mp"),
        P("mp"),
        P(None, None, "mp"),
        P(None, "mp"),
        P("mp"),
        P("mp"),
        P("mp"),
        P("mp"),
        P(None, "mp", None, None),
        P(None, None, "mp"),
        P(None, None, None, "mp"),
        P(),
        P(),
        P(),
    )
    return jax.shard_map(
        per_device, mesh=mesh, in_specs=placed, out_specs=P("seq", "mp"), check_vma=False
    )
```

profile of v0, /device:TPU:1, one launch (start us, length us, event | category | flops | bytes accessed | tf_op | source)
XLA Modules:
  0.0 195.6 jit_solution(3872452470648923946)
XLA Ops:
  8.4 17.2 %copy.111 = bf16[512,8,2,1024]{3,1,2,0:T(8,128)(2,1)} copy(bf16[512,8,2,1024]{3,2,1,0:T(2,128)(2,1)} %bitcast.142) | data formatting | bytes 33554432
  26.2 34.1 %all-gather.2.cloned.1.call-done = bf16[512,4096]{1,0:T(8,128)(2,1)} async-done(((bf16[512,1024]{1,0:T(8,128)(2,1)}), bf16[512,4096]{1,0:T(8,128)(2,1)}) %all-gather.2.cloned.1.call-update) | async-done | bytes 4194320 | tf_op jit(solution)/shard_map/all_gather | solution.py:57
  60.3 15.8 %convolution_convert_fusion = bf16[512,2048]{1,0:T(8,128)(2,1)S(1)} fusion(bf16[512,4096]{1,0:T(8,128)(2,1)} %all-gather.2.cloned.1.call-done, bf16[4096,2048]{1,0:T(8,128)(2,1)} %bitcast.143), kind=kOutput, calls=%fused_computation.8 | convolution fusion | flops 8590983168 | bytes 23068672 | tf_op jit(solution)/shard_map/dot_general | solution.py:58
  76.2 2.2 %copy-done.16 = bf16[4096,2,128]{2,1,0:T(2,128)(2,1)S(1)} copy-done((bf16[4096,2,128]{2,1,0:T(2,128)(2,1)S(1)}, bf16[4096,2,128]{2,1,0:T(2,128)(2,1)}, u32[]{:S(2)}) %copy-start.16) | copy-done | bytes 2097176
  79.9 2.1 %collective-permute-start = (bf16[2,3,1280]{2,0,1:T(2,128)(2,1)S(1)}, bf16[2,3,1280]{2,0,1:T(2,128)(2,1)S(1)}, u32[]{:S(2)}, u32[]{:S(2)}) collective-permute-start(bf16[2,3,1280]{2,0,1:T(2,128)(2,1)S(1)} %copy.107), channel_id=1, source_target_pairs={{0,4},{4,8},{8,12},{12,16},{16,20},{20,24},{24,28},{28,32},{32,36}... | collective-permute-start | bytes 46088 | tf_op jit(solution)/shard_map/ppermute | solution.py:17
  89.5 1.7 multiply_convert_fusion.2
  92.6 2.3 %copy.84 = bf16[2,256,1024]{1,2,0:T(8,128)(2,1)} copy(bf16[2,256,1024]{2,1,0:T(8,128)(2,1)} %get-tuple-element.33) | data formatting | bytes 2097152 | tf_op jit(solution)/shard_map/slice | solution.py:95
  96.6 4.6 %copy_add_fusion = (f32[2,16,64,128]{3,0,2,1:T(2,128)S(1)}, f32[2,16,64,128]{3,0,2,1:T(2,128)}) fusion(f32[2,16,64,128]{3,2,1,0:T(8,128)S(1)} %fusion.23, pred[2]{0:T(512)(128)(4,1)S(1)} %compare_reduce_fusion, f32[2,16]{0,1:T(8,128)S(1)} %copy.89, f32[2,16,64,128]{3,2,1,0:T(8,128)S(1)} %copy-done, s32[2]{0:T(128)S(1)} %fusion.46), kind=kOutput, calls=%fused_computation.42 | convolution fusion | flops 7077892 | bytes 4194442 | tf_op jit(solution)/shard_map/cr,rhpn->chpn/dot_general | solution.py:82
  102.2 2.5 %collective-permute-start.3 = (f32[8]{0:T(128)S(1)}, f32[8]{0:T(128)S(1)}, u32[]{:S(2)}, u32[]{:S(2)}) collective-permute-start(f32[8]{0:T(128)S(1)} %get-tuple-element.18), channel_id=1, source_target_pairs={{0,16},{4,20},{8,24},{12,28},{16,32},{20,36},{24,40},{28,44},{32,4... | collective-permute-start | bytes 104 | tf_op jit(solution)/shard_map/ppermute | solution.py:17
  106.2 2.1 %collective-permute-done.3 = f32[8]{0:T(128)S(1)} collective-permute-done((f32[8]{0:T(128)S(1)}, f32[8]{0:T(128)S(1)}, u32[]{:S(2)}, u32[]{:S(2)}) %collective-permute-start.3) | collective-permute-done | bytes 64 | tf_op jit(solution)/shard_map/ppermute | solution.py:17
  113.6 4.8 %collective-permute-done.6 = f32[8,64,128]{2,1,0:T(8,128)S(1)} collective-permute-done((f32[8,64,128]{2,1,0:T(8,128)S(1)}, f32[8,64,128]{2,1,0:T(8,128)S(1)}, u32[]{:S(2)}, u32[]{:S(2)}) %collective-permute-start.6) | collective-permute-done | bytes 262176 | tf_op jit(solution)/shard_map/ppermute | solution.py:17
  119.8 4.0 %collective-permute-done.14 = f32[8,64,128]{2,1,0:T(8,128)S(1)} collective-permute-done((f32[8,64,128]{2,1,0:T(8,128)S(1)}, f32[8,64,128]{2,1,0:T(8,128)S(1)}, u32[]{:S(2)}, u32[]{:S(2)}) %collective-permute-start.14) | collective-permute-done | bytes 262176 | tf_op jit(solution)/shard_map/ppermute | solution.py:17
  124.2 4.8 %collective-permute-done.7 = f32[8,64,128]{2,1,0:T(8,128)S(1)} collective-permute-done((f32[8,64,128]{2,1,0:T(8,128)S(1)}, f32[8,64,128]{2,1,0:T(8,128)S(1)}, u32[]{:S(2)}, u32[]{:S(2)}) %collective-permute-start.7) | collective-permute-done | bytes 262176 | tf_op jit(solution)/shard_map/ppermute | solution.py:17
  129.3 5.3 %collective-permute-done.15 = f32[8,64,128]{2,1,0:T(8,128)S(1)} collective-permute-done((f32[8,64,128]{2,1,0:T(8,128)S(1)}, f32[8,64,128]{2,1,0:T(8,128)S(1)}, u32[]{:S(2)}, u32[]{:S(2)}) %collective-permute-start.15) | collective-permute-done | bytes 262176 | tf_op jit(solution)/shard_map/ppermute | solution.py:17
  137.3 5.9 %collective-permute-done.16 = f32[8,64,128]{2,1,0:T(8,128)S(1)} collective-permute-done((f32[8,64,128]{2,1,0:T(8,128)S(1)}, f32[8,64,128]{2,1,0:T(8,128)S(1)}, u32[]{:S(2)}, u32[]{:S(2)}) %collective-permute-start.16) | collective-permute-done | bytes 262176 | tf_op jit(solution)/shard_map/ppermute | solution.py:17
  143.7 3.7 %collective-permute-done.9 = f32[8,64,128]{2,1,0:T(8,128)S(1)} collective-permute-done((f32[8,64,128]{2,1,0:T(8,128)S(1)}, f32[8,64,128]{2,1,0:T(8,128)S(1)}, u32[]{:S(2)}, u32[]{:S(2)}) %collective-permute-start.9) | collective-permute-done | bytes 262176 | tf_op jit(solution)/shard_map/ppermute | solution.py:17
  147.7 5.8 %collective-permute-done.17 = f32[8,64,128]{2,1,0:T(8,128)S(1)} collective-permute-done((f32[8,64,128]{2,1,0:T(8,128)S(1)}, f32[8,64,128]{2,1,0:T(8,128)S(1)}, u32[]{:S(2)}, u32[]{:S(2)}) %collective-permute-start.17) | collective-permute-done | bytes 262176 | tf_op jit(solution)/shard_map/ppermute | solution.py:17
  155.1 10.9 %collective-permute-start.19 = (f32[16,64,128]{2,1,0:T(8,128)}, f32[16,64,128]{2,1,0:T(8,128)}, u32[]{:S(2)}, u32[]{:S(2)}) collective-permute-start(f32[16,64,128]{2,1,0:T(8,128)} %get-tuple-element.31), channel_id=1, source_target_pairs={{0,4},{4,0},{8,12},{12,8},{16,20},{20,16},{24,28},{28,24},{32,36},... | collective-permute-start | bytes 1572872 | tf_op jit(solution)/shard_map/ppermute | solution.py:175
  166.0 1.8 copy.98
  173.0 2.1 %fusion.25 = f32[2,16,64,256]{3,2,1,0:T(8,128)S(1)} fusion(f32[2,16,64,128]{3,0,2,1:T(2,128)S(1)} %fusion.24, bf16[2,256,1280]{2,1,0:T(8,128)(2,1)} %copy-done.1), kind=kOutput, calls=%fused_computation.40 | convolution fusion | flops 805306368 | bytes 3276800 | tf_op jit(solution)/shard_map/cqgn,cgjpn->cqgjp/dot_general | solution.py:184
  175.0 2.6 %fusion.19 = f32[2,256,1,16,64]{1,4,3,0,2:T(8,128)S(1)} fusion(f32[2,16,64,256]{3,2,1,0:T(8,128)S(1)} %fusion.25, f32[2,256,1,16,64]{1,4,3,0,2:T(8,128)S(1)} %bitcast.149, bf16[2,256,16,64]{1,3,2,0:T(8,128)(2,1)S(1)} %bitcast.147, f32[2,16,256]{2,1,0:T(8,128)S(1)} %get-tuple-element.42, f32[2,16,256]{2,1,0:T(8,128)S(1)} %get-tuple-element.45, ...), kind=kOutput, calls=%fused_computation.30 | convolution fusion | flops 281018368 | bytes 8028224 | tf_op jit(solution)/shard_map/cgjqk,ckgjp->cqgjp/dot_general | solution.py:109
  177.7 3.8 %copy.105 = f32[2,256,1,16,64]{4,3,1,0,2:T(8,128)} copy(f32[2,256,1,16,64]{1,4,3,0,2:T(8,128)S(1)} %fusion.19) | data formatting | bytes 4194304 | tf_op jit(solution)/shard_map/reshape | solution.py:193
  181.5 3.5 %reshape.290 = f32[512,1024]{1,0:T(8,128)S(1)} reshape(f32[2,256,1,16,64]{4,3,1,0,2:T(8,128)} %copy.105) | data formatting | bytes 4194304 | tf_op jit(solution)/shard_map/reshape | solution.py:193
  185.0 2.1 %multiply_reduce_fusion = f32[512]{0:T(512)S(1)} fusion(f32[512,1024]{1,0:T(8,128)S(1)} %reshape.290, bf16[512,2048]{1,0:T(8,128)(2,1)} %copy-done.2), kind=kLoop, calls=%fused_computation.32 | loop fusion | flops 4193792 | bytes 3147776 | tf_op jit(solution)/shard_map/reduce_sum | solution.py:195
  (156 shorter events, 35.8 us)
Async XLA Ops:
  6.5 90.0 %copy-start = (f32[2,16,64,128]{3,2,1,0:T(8,128)S(1)}, f32[2,16,64,128]{3,2,1,0:T(8,128)}, u32[]{:S(2)}) copy-start(f32[2,16,64,128]{3,2,1,0:T(8,128)} %param.30) | copy-start | bytes 3145732
  6.5 53.7 %all-gather.2.cloned.1.call-start = ((), (), s32[]{:S(2)}) async-start(), calls=%async_computation | async-start | bytes 5242880 | tf_op jit(solution)/shard_map/all_gather | solution.py:57
  8.4 17.7 %copy-start.12 = (f32[4,2,128]{2,1,0:T(2,128)S(1)}, f32[4,2,128]{2,1,0:T(2,128)}, u32[]{:S(2)}) copy-start(f32[4,2,128]{2,1,0:T(2,128)} %param.24) | copy-start | bytes 12292
  8.4 17.8 %copy-start.18 = (f32[16]{0:T(128)S(1)}, f32[16]{0:T(128)}, u32[]{:S(2)}) copy-start(f32[16]{0:T(128)} %param.26) | copy-start | bytes 196
  79.9 9.1 %collective-permute-start = (bf16[2,3,1280]{2,0,1:T(2,128)(2,1)S(1)}, bf16[2,3,1280]{2,0,1:T(2,128)(2,1)S(1)}, u32[]{:S(2)}, u32[]{:S(2)}) collective-permute-start(bf16[2,3,1280]{2,0,1:T(2,128)(2,1)S(1)} %copy.107), channel_id=1, source_target_pairs={{0,4},{4,8},{8,12},{12,16},{16,20},{20,24},{24,28},{28,32},{32,36}... | collective-permute-start | bytes 46088 | tf_op jit(solution)/shard_map/ppermute | solution.py:17
  85.3 1.2 collective-permute-start.1
  86.7 15.5 %collective-permute-start.2 = (f32[8]{0:T(128)S(1)}, f32[8]{0:T(128)S(1)}, u32[]{:S(2)}, u32[]{:S(2)}) collective-permute-start(f32[8]{0:T(128)S(1)} %reshape_squeeze.12), channel_id=1, source_target_pairs={{0,8},{4,12},{8,16},{12,20},{16,24},{20,28},{24,32},{28,36},{32,40... | collective-permute-start | bytes 104 | tf_op jit(solution)/shard_map/ppermute | solution.py:17
  88.0 16.7 %collective-permute-start.11 = (f32[8]{0:T(128)S(1)}, f32[8]{0:T(128)S(1)}, u32[]{:S(2)}, u32[]{:S(2)}) collective-permute-start(f32[8]{0:T(128)S(1)} %reshape_squeeze.14), channel_id=1, source_target_pairs={{0,8},{4,12},{8,16},{12,20},{16,24},{20,28},{24,32},{28,36},{32,40... | collective-permute-start | bytes 104 | tf_op jit(solution)/shard_map/ppermute | solution.py:17
  101.3 7.1 %collective-permute-start.5 = (f32[16,64,128]{2,1,0:T(8,128)S(1)}, f32[16,64,128]{2,1,0:T(8,128)S(1)}, u32[]{:S(2)}, u32[]{:S(2)}) collective-permute-start(f32[16,64,128]{2,1,0:T(8,128)S(1)} %bitcast.155), channel_id=1, source_target_pairs={{0,4},{4,0},{8,12},{12,8},{16,20},{20,16},{24,28},{28,24},{32,36},... | collective-permute-start | bytes 1572872 | tf_op jit(solution)/shard_map/ppermute | solution.py:133
  102.2 6.0 %collective-permute-start.3 = (f32[8]{0:T(128)S(1)}, f32[8]{0:T(128)S(1)}, u32[]{:S(2)}, u32[]{:S(2)}) collective-permute-start(f32[8]{0:T(128)S(1)} %get-tuple-element.18), channel_id=1, source_target_pairs={{0,16},{4,20},{8,24},{12,28},{16,32},{20,36},{24,40},{28,44},{32,4... | collective-permute-start | bytes 104 | tf_op jit(solution)/shard_map/ppermute | solution.py:17
  104.8 6.0 %collective-permute-start.12 = (f32[8]{0:T(128)S(1)}, f32[8]{0:T(128)S(1)}, u32[]{:S(2)}, u32[]{:S(2)}) collective-permute-start(f32[8]{0:T(128)S(1)} %get-tuple-element.25), channel_id=1, source_target_pairs={{0,16},{4,20},{8,24},{12,28},{16,32},{20,36},{24,40},{28,44},{32,4... | collective-permute-start | bytes 104 | tf_op jit(solution)/shard_map/ppermute | solution.py:17
  108.3 3.6 %collective-permute-start.4 = (f32[8]{0:T(128)S(1)}, f32[8]{0:T(128)S(1)}, u32[]{:S(2)}, u32[]{:S(2)}) collective-permute-start(f32[8]{0:T(128)S(1)} %fusion.58), channel_id=1, source_target_pairs={{0,32},{4,36},{8,40},{12,44},{16,48},{20,52},{24,56},{28,60},{32,6... | collective-permute-start | bytes 104 | tf_op jit(solution)/shard_map/ppermute | solution.py:17
  108.6 9.8 %collective-permute-start.6 = (f32[8,64,128]{2,1,0:T(8,128)S(1)}, f32[8,64,128]{2,1,0:T(8,128)S(1)}, u32[]{:S(2)}, u32[]{:S(2)}) collective-permute-start(f32[8,64,128]{2,1,0:T(8,128)S(1)} %bitcast.154), channel_id=1, source_target_pairs={{0,8},{4,12},{8,16},{12,20},{16,24},{20,28},{24,32},{28,36},{32,40... | collective-permute-start | bytes 786440 | tf_op jit(solution)/shard_map/ppermute | solution.py:17
  110.9 7.7 %collective-permute-start.13 = (f32[8]{0:T(128)S(1)}, f32[8]{0:T(128)S(1)}, u32[]{:S(2)}, u32[]{:S(2)}) collective-permute-start(f32[8]{0:T(128)S(1)} %fusion.60), channel_id=1, source_target_pairs={{0,32},{4,36},{8,40},{12,44},{16,48},{20,52},{24,56},{28,60},{32,6... | collective-permute-start | bytes 104 | tf_op jit(solution)/shard_map/ppermute | solution.py:17
  112.0 17.1 %collective-permute-start.10 = (f32[8]{0:T(128)S(1)}, f32[8]{0:T(128)S(1)}, u32[]{:S(2)}, u32[]{:S(2)}) collective-permute-start(f32[8]{0:T(128)S(1)} %fusion.53), channel_id=1, source_target_pairs={{0,64},{4,68},{8,72},{12,76},{16,80},{20,84},{24,88},{28,92},{32,9... | collective-permute-start | bytes 104 | tf_op jit(solution)/shard_map/ppermute | solution.py:17
  113.6 10.3 %collective-permute-start.14 = (f32[8,64,128]{2,1,0:T(8,128)S(1)}, f32[8,64,128]{2,1,0:T(8,128)S(1)}, u32[]{:S(2)}, u32[]{:S(2)}) collective-permute-start(f32[8,64,128]{2,1,0:T(8,128)S(1)} %bitcast.153), channel_id=1, source_target_pairs={{0,8},{4,12},{8,16},{12,20},{16,24},{20,28},{24,32},{28,36},{32,40... | collective-permute-start | bytes 786440 | tf_op jit(solution)/shard_map/ppermute | solution.py:17
  118.5 10.5 %collective-permute-start.7 = (f32[8,64,128]{2,1,0:T(8,128)S(1)}, f32[8,64,128]{2,1,0:T(8,128)S(1)}, u32[]{:S(2)}, u32[]{:S(2)}) collective-permute-start(f32[8,64,128]{2,1,0:T(8,128)S(1)} %multiply_add_fusion.5), channel_id=1, source_target_pairs={{0,16},{4,20},{8,24},{12,28},{16,32},{20,36},{24,40},{28,44},{32,4... | collective-permute-start | bytes 786440 | tf_op jit(solution)/shard_map/ppermute | solution.py:17
  118.7 18.4 %collective-permute-start.18 = (f32[8]{0:T(128)S(1)}, f32[8]{0:T(128)S(1)}, u32[]{:S(2)}, u32[]{:S(2)}) collective-permute-start(f32[8]{0:T(128)S(1)} %fusion.55), channel_id=1, source_target_pairs={{0,64},{4,68},{8,72},{12,76},{16,80},{20,84},{24,88},{28,92},{32,9... | collective-permute-start | bytes 104 | tf_op jit(solution)/shard_map/ppermute | solution.py:17
  124.0 10.6 %collective-permute-start.15 = (f32[8,64,128]{2,1,0:T(8,128)S(1)}, f32[8,64,128]{2,1,0:T(8,128)S(1)}, u32[]{:S(2)}, u32[]{:S(2)}) collective-permute-start(f32[8,64,128]{2,1,0:T(8,128)S(1)} %multiply_add_fusion.2), channel_id=1, source_target_pairs={{0,16},{4,20},{8,24},{12,28},{16,32},{20,36},{24,40},{28,44},{32,4... | collective-permute-start | bytes 786440 | tf_op jit(solution)/shard_map/ppermute | solution.py:17
  129.1 6.5 %collective-permute-start.8 = (f32[8,64,128]{2,1,0:T(8,128)S(1)}, f32[8,64,128]{2,1,0:T(8,128)S(1)}, u32[]{:S(2)}, u32[]{:S(2)}) collective-permute-start(f32[8,64,128]{2,1,0:T(8,128)S(1)} %multiply_add_fusion.4), channel_id=1, source_target_pairs={{0,32},{4,36},{8,40},{12,44},{16,48},{20,52},{24,56},{28,60},{32,6... | collective-permute-start | bytes 786440 | tf_op jit(solution)/shard_map/ppermute | solution.py:17
  134.7 8.6 %collective-permute-start.16 = (f32[8,64,128]{2,1,0:T(8,128)S(1)}, f32[8,64,128]{2,1,0:T(8,128)S(1)}, u32[]{:S(2)}, u32[]{:S(2)}) collective-permute-start(f32[8,64,128]{2,1,0:T(8,128)S(1)} %multiply_add_fusion.1), channel_id=1, source_target_pairs={{0,32},{4,36},{8,40},{12,44},{16,48},{20,52},{24,56},{28,60},{32,6... | collective-permute-start | bytes 786440 | tf_op jit(solution)/shard_map/ppermute | solution.py:17
  135.7 11.7 %collective-permute-start.9 = (f32[8,64,128]{2,1,0:T(8,128)S(1)}, f32[8,64,128]{2,1,0:T(8,128)S(1)}, u32[]{:S(2)}, u32[]{:S(2)}) collective-permute-start(f32[8,64,128]{2,1,0:T(8,128)S(1)} %multiply_add_fusion.3), channel_id=1, source_target_pairs={{0,64},{4,68},{8,72},{12,76},{16,80},{20,84},{24,88},{28,92},{32,9... | collective-permute-start | bytes 786440 | tf_op jit(solution)/shard_map/ppermute | solution.py:17
  143.4 10.2 %collective-permute-start.17 = (f32[8,64,128]{2,1,0:T(8,128)S(1)}, f32[8,64,128]{2,1,0:T(8,128)S(1)}, u32[]{:S(2)}, u32[]{:S(2)}) collective-permute-start(f32[8,64,128]{2,1,0:T(8,128)S(1)} %multiply_add_fusion), channel_id=1, source_target_pairs={{0,64},{4,68},{8,72},{12,76},{16,80},{20,84},{24,88},{28,92},{32,9... | collective-permute-start | bytes 786440 | tf_op jit(solution)/shard_map/ppermute | solution.py:17
  155.1 15.5 %collective-permute-start.19 = (f32[16,64,128]{2,1,0:T(8,128)}, f32[16,64,128]{2,1,0:T(8,128)}, u32[]{:S(2)}, u32[]{:S(2)}) collective-permute-start(f32[16,64,128]{2,1,0:T(8,128)} %get-tuple-element.31), channel_id=1, source_target_pairs={{0,4},{4,0},{8,12},{12,8},{16,20},{20,16},{24,28},{28,24},{32,36},... | collective-permute-start | bytes 1572872 | tf_op jit(solution)/shard_map/ppermute | solution.py:175
  (17 other events, 121.7 us)
Sparse Core Ops, SparseCore 0:
  9.0 51.2 all-gather.1
where the time goes:
time: 196 us
  waiting for transfers between devices  75.5 us (39%)
  local copies, waits for them, and re-layouts  35.3 us (18%)
  matrix products  30.7 us (16%)
  starting transfers between devices  25.8 us (13%)
  other arithmetic  14.2 us (7%)
  between operations  14.1 us (7%)
    ppermute x17, waiting for transfers between devices, from_behind(): return lax.ppermute(value, axis, pairs)  39.6 us
    all_gather x1, waiting for transfers between devices, per_device(): piece = lax.all_gather(hidden, 'mp', axis=1, tiled=True)  34.1 us
    unnamed x44, local copies, waits for them, and re-layouts  19.5 us
    dot_general x1, matrix products, per_device(): zx_sum = jnp.dot(piece, flat_zx, preferred_element_type=jnp.float32)  15.8 us
    ppermute x17, starting transfers between devices, from_behind(): return lax.ppermute(value, axis, pairs)  14.1 us
    ppermute x1, starting transfers between devices, per_device(): lax.ppermute(jnp.where(core == 0, after_early, before_chip), 'seq', pair)  10.9 us
    reshape x2, local copies, waits for them, and re-layouts, per_device(): y_total.reshape(rows_dev, inner_dev) * jax.nn.silu(gate.astype(jnp.float32))  7.29 us
    dot_general x1, matrix products, per_device(): jnp.einsum('cr,rhpn->chpn', pick, state_bank, precision=lax.Precision.HIG...  4.63 us
  transfers between devices with their start and end apart: 21, of which 13 were waited for; matrix products, arithmetic and copies ran while one was open for 21% of the time, Pallas kernels for 0%

commit v1 on v0

--- a/solution.py
+++ b/solution.py
@@ -54,7 +54,9 @@
     prompts = prompt_blocks.shape[0]
     flat_zx = w_zx.reshape(WIDTH, 2 * inner_dev)
     flat_bc = w_bc.reshape(WIDTH, 2 * gstate_dev)
-    piece = lax.all_gather(hidden, "mp", axis=1, tiled=True)
+    size = lax.axis_size("mp")
+    repeats = [size if d == 1 else 1 for d in range(hidden.ndim)]
+    piece = lax.all_to_all(jnp.tile(hidden, repeats), "mp", split_axis=1, concat_axis=1, tiled=True)
     zx_sum = jnp.dot(piece, flat_zx, preferred_element_type=jnp.float32)
     bc_sum = jnp.dot(piece, flat_bc, preferred_element_type=jnp.float32)
     dt_raw = jnp.dot(piece, w_dt, preferred_element_type=jnp.float32)

time: 196 us -> 214 us (1.092)
  local copies, waits for them, and re-layouts: 35.3 us -> 60.6 us
  between operations: 14.1 us -> 0.7 us
  starting transfers between devices: 25.8 us -> 29.1 us
  matrix products: 30.7 us -> 33 us
    all_gather x1 -> x0, waiting for transfers between devices: 34.1 us -> none  [per_device(): piece = lax.all_gather(hidden, 'mp', axis=1, tiled=True)]
    all_to_all x0 -> x1, waiting for transfers between devices: none -> 30.8 us  [per_device(): lax.all_to_all(jnp.tile(hidden, repeats), 'mp', split_axis=1, concat_axis...]
    all_to_all x0 -> x2, local copies, waits for them, and re-layouts: none -> 13.6 us  [per_device(): lax.all_to_all(jnp.tile(hidden, repeats), 'mp', split_axis=1, concat_axis...]
    dot_general x0 -> x1, local copies, waits for them, and re-layouts: none -> 7.85 us  [per_device(): dt_raw = jnp.dot(piece, w_dt, preferred_element_type=jnp.float32)]
    ppermute x17, waiting for transfers between devices: 39.6 us -> 45.1 us  [from_behind(): return lax.ppermute(value, axis, pairs)]
    all_to_all x0 -> x1, starting transfers between devices: none -> 5.13 us  [per_device(): lax.all_to_all(jnp.tile(hidden, repeats), 'mp', split_axis=1, concat_axis...]
    ppermute x17, starting transfers between devices: 14.1 us -> 9 us  [from_behind(): return lax.ppermute(value, axis, pairs)]
    ppermute x2, starting transfers between devices: 0.8 us -> 4.78 us  [per_device(): lax.ppermute((keep(step_a, 1 - core), keep(step_b, 1 - core)), 'seq', pair)]
  transfers between devices with their start and end apart: 21 -> 21, of which waited for: 13 -> 11; matrix products, arithmetic and copies ran while one was open for 21% -> 29% of each run, Pallas kernels for 0% -> 0%
where the time goes in v1:
time: 214 us; the launch traced here: 213 us
  waiting for transfers between devices  75.9 us (35%)
  local copies, waits for them, and re-layouts  60.6 us (28%)
  matrix products  33 us (15%)
  starting transfers between devices  29.1 us (14%)
  other arithmetic  13.5 us (6%)
    ppermute x17, waiting for transfers between devices, from_behind(): return lax.ppermute(value, axis, pairs)  45.1 us
    all_to_all x1, waiting for transfers between devices, per_device(): lax.all_to_all(jnp.tile(hidden, repeats), 'mp', split_axis=1, concat_axis...  30.8 us
    unnamed x50, local copies, waits for them, and re-layouts  19.5 us
    dot_general x1, matrix products, per_device(): zx_sum = jnp.dot(piece, flat_zx, preferred_element_type=jnp.float32)  15.8 us
    all_to_all x2, local copies, waits for them, and re-layouts, per_device(): lax.all_to_all(jnp.tile(hidden, repeats), 'mp', split_axis=1, concat_axis...  13.6 us
    ppermute x1, starting transfers between devices, per_device(): lax.ppermute(jnp.where(core == 0, after_early, before_chip), 'seq', pair)  10.2 us
    ppermute x17, starting transfers between devices, from_behind(): return lax.ppermute(value, axis, pairs)  9 us
    dot_general x1, local copies, waits for them, and re-layouts, per_device(): dt_raw = jnp.dot(piece, w_dt, preferred_element_type=jnp.float32)  7.85 us
  transfers between devices with their start and end apart: 21, of which 11 were waited for; matrix products, arithmetic and copies ran while one was open for 29% of the time, Pallas kernels for 0%

profile of v1, /device:TPU:1, one launch (start us, length us, event | category | flops | bytes accessed | tf_op | source)
XLA Modules:
  0.0 212.8 jit_solution(6849377573275255118)
XLA Ops:
  0.0 3.8 %tile.2 = bf16[512,4,1024]{2,0,1:T(8,128)(2,1)} broadcast(bf16[512,1024]{1,0:T(8,128)(2,1)} %param.18), dimensions={0,2} | broadcast | bytes 5242880 | tf_op jit(solution)/shard_map/tile | solution.py:59
  3.9 5.1 %all-to-all-start = ((bf16[512,4,1024]{2,0,1:T(8,128)(2,1)}), bf16[512,4,1024]{2,0,1:T(8,128)(2,1)}, u32[]{:S(2)}, u32[]{:S(2)}) async-start(bf16[512,4,1024]{2,0,1:T(8,128)(2,1)} %tile.2), calls=%async_computation | async-start | bytes 8388608 | tf_op jit(solution)/shard_map/all_to_all | solution.py:59
  9.4 17.1 %copy.127 = bf16[512,8,2,1024]{3,1,2,0:T(8,128)(2,1)} copy(bf16[512,8,2,1024]{3,2,1,0:T(2,128)(2,1)} %bitcast.148) | data formatting | bytes 33554432
  27.1 30.8 %all-to-all-done = bf16[512,4,1024]{2,0,1:T(8,128)(2,1)} async-done(((bf16[512,4,1024]{2,0,1:T(8,128)(2,1)}), bf16[512,4,1024]{2,0,1:T(8,128)(2,1)}, u32[]{:S(2)}, u32[]{:S(2)}) %all-to-all-start) | async-done | bytes 4194336 | tf_op jit(solution)/shard_map/all_to_all | solution.py:59
  57.9 7.4 %copy.102 = bf16[512,4,1024]{2,1,0:T(4,128)(2,1)} copy(bf16[512,4,1024]{2,0,1:T(8,128)(2,1)} %all-to-all-done) | data formatting | bytes 8388608 | tf_op jit(solution)/shard_map/all_to_all | solution.py:59
  65.4 7.9 %dot_general.37 = bf16[2,256,4096]{2,1,0:T(8,128)(2,1)} reshape(bf16[512,4,1024]{2,1,0:T(4,128)(2,1)} %copy.102) | data formatting | bytes 8388608 | tf_op jit(solution)/shard_map/dot_general | solution.py:62
  73.2 3.4 %convolution_add_fusion = f32[2,256,16]{1,2,0:T(8,128)S(1)} fusion(bf16[2,256,4096]{2,1,0:T(8,128)(2,1)} %dot_general.37, bf16[4096,16]{0,1:T(8,128)(2,1)S(1)} %copy-done.8, f32[16]{0:T(128)S(1)} %copy-done.14), kind=kOutput, calls=%fused_computation.37 | convolution fusion | flops 67117056 | bytes 4358208 | tf_op jit(solution)/shard_map/dot_general | solution.py:62
  80.3 6.2 %copy.97 = bf16[512,4,1024]{0,2,1:T(8,128)(2,1)} copy(bf16[512,4,1024]{2,0,1:T(8,128)(2,1)} %all-to-all-done) | data formatting | bytes 8388608 | tf_op jit(solution)/shard_map/all_to_all | solution.py:59
  86.5 15.8 %convolution_convert_fusion = bf16[512,2048]{1,0:T(8,128)(2,1)S(1)} fusion(bf16[512,4096]{0,1:T(8,128)(2,1)} %bitcast.152, bf16[4096,2048]{1,0:T(8,128)(2,1)} %bitcast.149), kind=kOutput, calls=%fused_computation.8 | convolution fusion | flops 8590983168 | bytes 23068672 | tf_op jit(solution)/shard_map/dot_general | solution.py:60
  118.8 4.6 %copy_add_fusion = (f32[2,16,64,128]{3,0,2,1:T(2,128)S(1)}, f32[2,16,64,128]{3,0,2,1:T(2,128)}) fusion(f32[2,16,64,128]{3,2,1,0:T(8,128)S(1)} %fusion.23, pred[2]{0:T(512)(128)(4,1)S(1)} %compare_reduce_fusion, f32[2,16]{0,1:T(8,128)S(1)} %copy.106, f32[2,16,64,128]{3,2,1,0:T(8,128)S(1)} %copy-done, s32[2]{0:T(128)S(1)} %fusion.52), kind=kOutput, calls=%fused_computation.43 | convolution fusion | flops 7077892 | bytes 4194442 | tf_op jit(solution)/shard_map/cr,rhpn->chpn/dot_general | solution.py:84
  123.5 3.2 %collective-permute-start.5 = (f32[16,64,128]{2,1,0:T(8,128)S(1)}, f32[16,64,128]{2,1,0:T(8,128)S(1)}, u32[]{:S(2)}, u32[]{:S(2)}) collective-permute-start(f32[16,64,128]{2,1,0:T(8,128)S(1)} %bitcast.163), channel_id=1, source_target_pairs={{0,4},{4,0},{8,12},{12,8},{16,20},{20,16},{24,28},{28,24},{32,36},... | collective-permute-start | bytes 1572872 | tf_op jit(solution)/shard_map/ppermute | solution.py:135
  128.6 4.3 %collective-permute-done.3 = f32[8]{0:T(128)S(1)} collective-permute-done((f32[8]{0:T(128)S(1)}, f32[8]{0:T(128)S(1)}, u32[]{:S(2)}, u32[]{:S(2)}) %collective-permute-start.3) | collective-permute-done | bytes 64 | tf_op jit(solution)/shard_map/ppermute | solution.py:17
  133.4 3.2 %collective-permute-done.4 = f32[8]{0:T(128)S(1)} collective-permute-done((f32[8]{0:T(128)S(1)}, f32[8]{0:T(128)S(1)}, u32[]{:S(2)}, u32[]{:S(2)}) %collective-permute-start.4) | collective-permute-done | bytes 64 | tf_op jit(solution)/shard_map/ppermute | solution.py:17
  137.3 6.0 %collective-permute-done.6 = f32[8,64,128]{2,1,0:T(8,128)S(1)} collective-permute-done((f32[8,64,128]{2,1,0:T(8,128)S(1)}, f32[8,64,128]{2,1,0:T(8,128)S(1)}, u32[]{:S(2)}, u32[]{:S(2)}) %collective-permute-start.6) | collective-permute-done | bytes 262176 | tf_op jit(solution)/shard_map/ppermute | solution.py:17
  143.6 5.4 %collective-permute-done.14 = f32[8,64,128]{2,1,0:T(8,128)S(1)} collective-permute-done((f32[8,64,128]{2,1,0:T(8,128)S(1)}, f32[8,64,128]{2,1,0:T(8,128)S(1)}, u32[]{:S(2)}, u32[]{:S(2)}) %collective-permute-start.14) | collective-permute-done | bytes 262176 | tf_op jit(solution)/shard_map/ppermute | solution.py:17
  149.1 4.3 %collective-permute-done.7 = f32[8,64,128]{2,1,0:T(8,128)S(1)} collective-permute-done((f32[8,64,128]{2,1,0:T(8,128)S(1)}, f32[8,64,128]{2,1,0:T(8,128)S(1)}, u32[]{:S(2)}, u32[]{:S(2)}) %collective-permute-start.7) | collective-permute-done | bytes 262176 | tf_op jit(solution)/shard_map/ppermute | solution.py:17
  153.7 5.4 %collective-permute-done.15 = f32[8,64,128]{2,1,0:T(8,128)S(1)} collective-permute-done((f32[8,64,128]{2,1,0:T(8,128)S(1)}, f32[8,64,128]{2,1,0:T(8,128)S(1)}, u32[]{:S(2)}, u32[]{:S(2)}) %collective-permute-start.15) | collective-permute-done | bytes 262176 | tf_op jit(solution)/shard_map/ppermute | solution.py:17
  161.9 6.4 %collective-permute-done.16 = f32[8,64,128]{2,1,0:T(8,128)S(1)} collective-permute-done((f32[8,64,128]{2,1,0:T(8,128)S(1)}, f32[8,64,128]{2,1,0:T(8,128)S(1)}, u32[]{:S(2)}, u32[]{:S(2)}) %collective-permute-start.16) | collective-permute-done | bytes 262176 | tf_op jit(solution)/shard_map/ppermute | solution.py:17
  168.5 3.5 %collective-permute-done.9 = f32[8,64,128]{2,1,0:T(8,128)S(1)} collective-permute-done((f32[8,64,128]{2,1,0:T(8,128)S(1)}, f32[8,64,128]{2,1,0:T(8,128)S(1)}, u32[]{:S(2)}, u32[]{:S(2)}) %collective-permute-start.9) | collective-permute-done | bytes 262176 | tf_op jit(solution)/shard_map/ppermute | solution.py:17
  172.3 6.0 %collective-permute-done.17 = f32[8,64,128]{2,1,0:T(8,128)S(1)} collective-permute-done((f32[8,64,128]{2,1,0:T(8,128)S(1)}, f32[8,64,128]{2,1,0:T(8,128)S(1)}, u32[]{:S(2)}, u32[]{:S(2)}) %collective-permute-start.17) | collective-permute-done | bytes 262176 | tf_op jit(solution)/shard_map/ppermute | solution.py:17
  179.8 10.2 %collective-permute-start.19 = (f32[16,64,128]{2,1,0:T(8,128)}, f32[16,64,128]{2,1,0:T(8,128)}, u32[]{:S(2)}, u32[]{:S(2)}) collective-permute-start(f32[16,64,128]{2,1,0:T(8,128)} %get-tuple-element.31), channel_id=1, source_target_pairs={{0,4},{4,0},{8,12},{12,8},{16,20},{20,16},{24,28},{28,24},{32,36},... | collective-permute-start | bytes 1572872 | tf_op jit(solution)/shard_map/ppermute | solution.py:177
  199.1 2.6 %fusion.19 = f32[2,256,1,16,64]{1,4,3,0,2:T(8,128)S(1)} fusion(f32[2,16,64,256]{3,2,1,0:T(8,128)S(1)} %fusion.25, f32[2,256,1,16,64]{1,4,3,0,2:T(8,128)S(1)} %bitcast.157, bf16[2,256,16,64]{1,3,2,0:T(8,128)(2,1)S(1)} %bitcast.155, f32[2,16,256]{2,1,0:T(8,128)S(1)} %get-tuple-element.46, f32[2,16,256]{2,1,0:T(8,128)S(1)} %get-tuple-element.44, ...), kind=kOutput, calls=%fused_computation.30 | convolution fusion | flops 281018368 | bytes 8028224 | tf_op jit(solution)/shard_map/cgjqk,ckgjp->cqgjp/dot_general | solution.py:111
  201.7 3.8 %copy.122 = f32[2,256,1,16,64]{4,3,1,0,2:T(8,128)} copy(f32[2,256,1,16,64]{1,4,3,0,2:T(8,128)S(1)} %fusion.19) | data formatting | bytes 4194304 | tf_op jit(solution)/shard_map/reshape | solution.py:195
  205.5 3.5 %reshape.297 = f32[512,1024]{1,0:T(8,128)S(1)} reshape(f32[2,256,1,16,64]{4,3,1,0,2:T(8,128)} %copy.122) | data formatting | bytes 4194304 | tf_op jit(solution)/shard_map/reshape | solution.py:195
  (166 shorter events, 42.3 us)
Async XLA Ops:
  0.0 118.8 %copy-start = (f32[2,16,64,128]{3,2,1,0:T(8,128)S(1)}, f32[2,16,64,128]{3,2,1,0:T(8,128)}, u32[]{:S(2)}) copy-start(f32[2,16,64,128]{3,2,1,0:T(8,128)} %param.30) | copy-start | bytes 3145732
  3.9 54.1 %all-to-all-start = ((bf16[512,4,1024]{2,0,1:T(8,128)(2,1)}), bf16[512,4,1024]{2,0,1:T(8,128)(2,1)}, u32[]{:S(2)}, u32[]{:S(2)}) async-start(bf16[512,4,1024]{2,0,1:T(8,128)(2,1)} %tile.2), calls=%async_computation | async-start | bytes 8388608 | tf_op jit(solution)/shard_map/all_to_all | solution.py:59
  9.4 17.6 %copy-start.12 = (f32[4,2,128]{2,1,0:T(2,128)S(1)}, f32[4,2,128]{2,1,0:T(2,128)}, u32[]{:S(2)}) copy-start(f32[4,2,128]{2,1,0:T(2,128)} %param.24) | copy-start | bytes 12292
  9.4 17.7 %copy-start.21 = (f32[16]{0:T(128)S(1)}, f32[16]{0:T(128)}, u32[]{:S(2)}) copy-start(f32[16]{0:T(128)} %param.26) | copy-start | bytes 196
  78.6 29.3 %collective-permute-start.1 = (f32[16]{0:T(128)S(1)}, f32[16]{0:T(128)S(1)}, u32[]{:S(2)}, u32[]{:S(2)}) collective-permute-start(f32[16]{0:T(128)S(1)} %reshape.280), channel_id=1, source_target_pairs={{0,4},{4,0},{8,12},{12,8},{16,20},{20,16},{24,28},{28,24},{32,36},... | collective-permute-start | bytes 200 | tf_op jit(solution)/shard_map/ppermute | solution.py:135
  106.2 5.0 %collective-permute-start = (bf16[2,3,1280]{2,0,1:T(2,128)(2,1)S(1)}, bf16[2,3,1280]{2,0,1:T(2,128)(2,1)S(1)}, u32[]{:S(2)}, u32[]{:S(2)}) collective-permute-start(bf16[2,3,1280]{2,0,1:T(2,128)(2,1)S(1)} %copy.124), channel_id=1, source_target_pairs={{0,4},{4,8},{8,12},{12,16},{16,20},{20,24},{24,28},{28,32},{32,36}... | collective-permute-start | bytes 46088 | tf_op jit(solution)/shard_map/ppermute | solution.py:17
  108.1 18.6 %collective-permute-start.2 = (f32[8]{0:T(128)S(1)}, f32[8]{0:T(128)S(1)}, u32[]{:S(2)}, u32[]{:S(2)}) collective-permute-start(f32[8]{0:T(128)S(1)} %reshape_squeeze.12), channel_id=1, source_target_pairs={{0,8},{4,12},{8,16},{12,20},{16,24},{20,28},{24,32},{28,36},{32,40... | collective-permute-start | bytes 104 | tf_op jit(solution)/shard_map/ppermute | solution.py:17
  109.8 17.0 %collective-permute-start.11 = (f32[8]{0:T(128)S(1)}, f32[8]{0:T(128)S(1)}, u32[]{:S(2)}, u32[]{:S(2)}) collective-permute-start(f32[8]{0:T(128)S(1)} %reshape_squeeze.14), channel_id=1, source_target_pairs={{0,8},{4,12},{8,16},{12,20},{16,24},{20,28},{24,32},{28,36},{32,40... | collective-permute-start | bytes 104 | tf_op jit(solution)/shard_map/ppermute | solution.py:17
  123.5 9.4 %collective-permute-start.5 = (f32[16,64,128]{2,1,0:T(8,128)S(1)}, f32[16,64,128]{2,1,0:T(8,128)S(1)}, u32[]{:S(2)}, u32[]{:S(2)}) collective-permute-start(f32[16,64,128]{2,1,0:T(8,128)S(1)} %bitcast.163), channel_id=1, source_target_pairs={{0,4},{4,0},{8,12},{12,8},{16,20},{20,16},{24,28},{28,24},{32,36},... | collective-permute-start | bytes 1572872 | tf_op jit(solution)/shard_map/ppermute | solution.py:135
  126.8 6.0 %collective-permute-start.3 = (f32[8]{0:T(128)S(1)}, f32[8]{0:T(128)S(1)}, u32[]{:S(2)}, u32[]{:S(2)}) collective-permute-start(f32[8]{0:T(128)S(1)} %get-tuple-element.18), channel_id=1, source_target_pairs={{0,16},{4,20},{8,24},{12,28},{16,32},{20,36},{24,40},{28,44},{32,4... | collective-permute-start | bytes 104 | tf_op jit(solution)/shard_map/ppermute | solution.py:17
  126.9 6.4 %collective-permute-start.12 = (f32[8]{0:T(128)S(1)}, f32[8]{0:T(128)S(1)}, u32[]{:S(2)}, u32[]{:S(2)}) collective-permute-start(f32[8]{0:T(128)S(1)} %get-tuple-element.25), channel_id=1, source_target_pairs={{0,16},{4,20},{8,24},{12,28},{16,32},{20,36},{24,40},{28,44},{32,4... | collective-permute-start | bytes 104 | tf_op jit(solution)/shard_map/ppermute | solution.py:17
  132.9 3.6 %collective-permute-start.4 = (f32[8]{0:T(128)S(1)}, f32[8]{0:T(128)S(1)}, u32[]{:S(2)}, u32[]{:S(2)}) collective-permute-start(f32[8]{0:T(128)S(1)} %fusion.64), channel_id=1, source_target_pairs={{0,32},{4,36},{8,40},{12,44},{16,48},{20,52},{24,56},{28,60},{32,6... | collective-permute-start | bytes 104 | tf_op jit(solution)/shard_map/ppermute | solution.py:17
  133.2 10.1 %collective-permute-start.6 = (f32[8,64,128]{2,1,0:T(8,128)S(1)}, f32[8,64,128]{2,1,0:T(8,128)S(1)}, u32[]{:S(2)}, u32[]{:S(2)}) collective-permute-start(f32[8,64,128]{2,1,0:T(8,128)S(1)} %bitcast.162), channel_id=1, source_target_pairs={{0,8},{4,12},{8,16},{12,20},{16,24},{20,28},{24,32},{28,36},{32,40... | collective-permute-start | bytes 786440 | tf_op jit(solution)/shard_map/ppermute | solution.py:17
  133.3 10.1 %collective-permute-start.13 = (f32[8]{0:T(128)S(1)}, f32[8]{0:T(128)S(1)}, u32[]{:S(2)}, u32[]{:S(2)}) collective-permute-start(f32[8]{0:T(128)S(1)} %fusion.66), channel_id=1, source_target_pairs={{0,32},{4,36},{8,40},{12,44},{16,48},{20,52},{24,56},{28,60},{32,6... | collective-permute-start | bytes 104 | tf_op jit(solution)/shard_map/ppermute | solution.py:17
  136.6 17.0 %collective-permute-start.10 = (f32[8]{0:T(128)S(1)}, f32[8]{0:T(128)S(1)}, u32[]{:S(2)}, u32[]{:S(2)}) collective-permute-start(f32[8]{0:T(128)S(1)} %fusion.59), channel_id=1, source_target_pairs={{0,64},{4,68},{8,72},{12,76},{16,80},{20,84},{24,88},{28,92},{32,9... | collective-permute-start | bytes 104 | tf_op jit(solution)/shard_map/ppermute | solution.py:17
  137.3 11.7 %collective-permute-start.14 = (f32[8,64,128]{2,1,0:T(8,128)S(1)}, f32[8,64,128]{2,1,0:T(8,128)S(1)}, u32[]{:S(2)}, u32[]{:S(2)}) collective-permute-start(f32[8,64,128]{2,1,0:T(8,128)S(1)} %bitcast.161), channel_id=1, source_target_pairs={{0,8},{4,12},{8,16},{12,20},{16,24},{20,28},{24,32},{28,36},{32,40... | collective-permute-start | bytes 786440 | tf_op jit(solution)/shard_map/ppermute | solution.py:17
  143.3 10.1 %collective-permute-start.7 = (f32[8,64,128]{2,1,0:T(8,128)S(1)}, f32[8,64,128]{2,1,0:T(8,128)S(1)}, u32[]{:S(2)}, u32[]{:S(2)}) collective-permute-start(f32[8,64,128]{2,1,0:T(8,128)S(1)} %multiply_add_fusion.5), channel_id=1, source_target_pairs={{0,16},{4,20},{8,24},{12,28},{16,32},{20,36},{24,40},{28,44},{32,4... | collective-permute-start | bytes 786440 | tf_op jit(solution)/shard_map/ppermute | solution.py:17
  143.5 18.1 %collective-permute-start.18 = (f32[8]{0:T(128)S(1)}, f32[8]{0:T(128)S(1)}, u32[]{:S(2)}, u32[]{:S(2)}) collective-permute-start(f32[8]{0:T(128)S(1)} %fusion.61), channel_id=1, source_target_pairs={{0,64},{4,68},{8,72},{12,76},{16,80},{20,84},{24,88},{28,92},{32,9... | collective-permute-start | bytes 104 | tf_op jit(solution)/shard_map/ppermute | solution.py:17
  149.0 10.1 %collective-permute-start.15 = (f32[8,64,128]{2,1,0:T(8,128)S(1)}, f32[8,64,128]{2,1,0:T(8,128)S(1)}, u32[]{:S(2)}, u32[]{:S(2)}) collective-permute-start(f32[8,64,128]{2,1,0:T(8,128)S(1)} %multiply_add_fusion.2), channel_id=1, source_target_pairs={{0,16},{4,20},{8,24},{12,28},{16,32},{20,36},{24,40},{28,44},{32,4... | collective-permute-start | bytes 786440 | tf_op jit(solution)/shard_map/ppermute | solution.py:17
  153.5 6.5 %collective-permute-start.8 = (f32[8,64,128]{2,1,0:T(8,128)S(1)}, f32[8,64,128]{2,1,0:T(8,128)S(1)}, u32[]{:S(2)}, u32[]{:S(2)}) collective-permute-start(f32[8,64,128]{2,1,0:T(8,128)S(1)} %multiply_add_fusion.4), channel_id=1, source_target_pairs={{0,32},{4,36},{8,40},{12,44},{16,48},{20,52},{24,56},{28,60},{32,6... | collective-permute-start | bytes 786440 | tf_op jit(solution)/shard_map/ppermute | solution.py:17
  159.3 9.0 %collective-permute-start.16 = (f32[8,64,128]{2,1,0:T(8,128)S(1)}, f32[8,64,128]{2,1,0:T(8,128)S(1)}, u32[]{:S(2)}, u32[]{:S(2)}) collective-permute-start(f32[8,64,128]{2,1,0:T(8,128)S(1)} %multiply_add_fusion.1), channel_id=1, source_target_pairs={{0,32},{4,36},{8,40},{12,44},{16,48},{20,52},{24,56},{28,60},{32,6... | collective-permute-start | bytes 786440 | tf_op jit(solution)/shard_map/ppermute | solution.py:17
  160.2 11.8 %collective-permute-start.9 = (f32[8,64,128]{2,1,0:T(8,128)S(1)}, f32[8,64,128]{2,1,0:T(8,128)S(1)}, u32[]{:S(2)}, u32[]{:S(2)}) collective-permute-start(f32[8,64,128]{2,1,0:T(8,128)S(1)} %multiply_add_fusion.3), channel_id=1, source_target_pairs={{0,64},{4,68},{8,72},{12,76},{16,80},{20,84},{24,88},{28,92},{32,9... | collective-permute-start | bytes 786440 | tf_op jit(solution)/shard_map/ppermute | solution.py:17
  168.4 9.9 %collective-permute-start.17 = (f32[8,64,128]{2,1,0:T(8,128)S(1)}, f32[8,64,128]{2,1,0:T(8,128)S(1)}, u32[]{:S(2)}, u32[]{:S(2)}) collective-permute-start(f32[8,64,128]{2,1,0:T(8,128)S(1)} %multiply_add_fusion), channel_id=1, source_target_pairs={{0,64},{4,68},{8,72},{12,76},{16,80},{20,84},{24,88},{28,92},{32,9... | collective-permute-start | bytes 786440 | tf_op jit(solution)/shard_map/ppermute | solution.py:17
  179.8 14.8 %collective-permute-start.19 = (f32[16,64,128]{2,1,0:T(8,128)}, f32[16,64,128]{2,1,0:T(8,128)}, u32[]{:S(2)}, u32[]{:S(2)}) collective-permute-start(f32[16,64,128]{2,1,0:T(8,128)} %get-tuple-element.31), channel_id=1, source_target_pairs={{0,4},{4,0},{8,12},{12,8},{16,20},{20,16},{24,28},{28,24},{32,36},... | collective-permute-start | bytes 1572872 | tf_op jit(solution)/shard_map/ppermute | solution.py:177
  (20 other events, 143.3 us)
